TPU v7x, 128 devices: a whole 4x4x4 slice. The times are simulated.
128 devices in a mesh: space: 64 (over y, z_hi, x, core), vec: 2 (over z_lo).
Axes of the slice: x: 4, y: 4, z: 4 (z_hi: 2, z_lo: 2; z = z_hi * 2 + z_lo), core: 2. Of those that a mesh axis runs over, the one named last changes fastest.
Arguments:
- potential: float32 [64, 128, 256], P('space'), may hold values from -8.25 to 8.25
- start_basis: float32 [16, 64, 128, 256], P('vec', 'space'), may hold values from -6 to 6
Outputs:
- new_basis: float32 [16, 64, 128, 256], P('vec', 'space')
- rayleigh: float32 [16, 16], replicated
All inputs are finite; a program needn't handle non-finite values.
Results may differ from a plain program's by a relative error of at most 0.0003.
Values sent between devices are 32-bit elements; how exact they have to be, the bound alone decides.
No kernel may reach another device: no remote copies, remote signals or barrier semaphores. Data moves between devices by JAX's collectives and lax.ppermute only.
A program may use at most 64 MiB of HBM per device.

v0:
```python
import jax
import jax.numpy as jnp
from jax import lax
from jax.sharding import PartitionSpec as P

NSWEEP = 3
SIGMA = 0.5
PREC = lax.Precision.HIGHEST


def extended(value, sides, width):
    for axis, dim in sides:
        peers, length = (lax.axis_size(axis), value.shape[dim])
        up = [(i, (i + 1) % peers) for i in range(peers)]
        down = [(j, i) for i, j in up]
        last = lax.slice_in_dim(value, length - width, length, axis=dim)
        first = lax.slice_in_dim(value, 0, width, axis=dim)
        before = lax.ppermute(last, axis, up)
        after = lax.ppermute(first, axis, down)
        value = jnp.concatenate([before, value, after], axis=dim)
    return value


def local_inner(left, right, scale):
    return jnp.einsum("kzyx,jzyx->kj", left, right, precision=PREC) * scale


def combine(coeff, vectors):
    return jnp.einsum("kj,kzyx->jzyx", coeff, vectors, precision=PREC)


def stencil(padded, potential):
    center = padded[:, 1:-1]
    beside = padded[:, 2:] + padded[:, :-2]
    beside = beside + jnp.roll(center, 1, 2) + jnp.roll(center, -1, 2)
    beside = beside + jnp.roll(center, 1, 3) + jnp.roll(center, -1, 3)
    return potential * center - beside


def inverse_factor(gram):
    lower = jnp.linalg.cholesky(gram)
    return jax.scipy.linalg.solve_triangular(
        lower, jnp.eye(gram.shape[0], dtype=jnp.float32), lower=True
    )


def local(potential, start_basis):
    mine = start_basis.shape[0]
    scale = 1.0 / (
        start_basis.shape[1] * start_basis.shape[2] * start_basis.shape[3] * lax.axis_size("space")
    )
    first = lax.axis_index("vec") * mine
    whole = lax.all_gather(start_basis, "vec", axis=0, tiled=True)
    gram = lax.psum(local_inner(whole, whole, scale), "space")
    basis_all = combine(inverse_factor(gram).T, whole)
    basis = lax.dynamic_slice_in_dim(basis_all, first, mine, 0)
    shifted = jnp.where(potential >= SIGMA, potential - SIGMA + 6.0, potential - SIGMA - 6.0)
    padded = extended(basis, (("space", 1),), 1)
    image = stencil(padded, potential)
    panel = lax.psum(local_inner(basis_all, image, scale), "space")
    rayleigh = lax.all_gather(panel, "vec", axis=1, tiled=True)
    panel_mine = lax.dynamic_slice_in_dim(rayleigh, first, mine, 1)
    resid = image - combine(panel_mine, basis_all)
    correction = jnp.zeros_like(basis)
    for sweep in range(NSWEEP):
        coeff = lax.psum(local_inner(basis_all, correction, scale), "space")
        proj = correction - combine(coeff, basis_all)
        padded = extended(proj, (("space", 1),), 1)
        moved = stencil(padded, potential) - SIGMA * proj
        back = lax.psum(local_inner(basis_all, moved, scale), "space")
        update = -resid - (moved - combine(back, basis_all))
        correction = correction + update / shifted
    proj_two = lax.psum(local_inner(basis_all, correction, scale), "space")
    fresh = correction - combine(proj_two, basis_all)
    fresh_all = lax.all_gather(fresh, "vec", axis=0, tiled=True)
    gram_two = lax.psum(local_inner(fresh_all, fresh_all, scale), "space")
    inverse_two = inverse_factor(gram_two)
    rows_mine = lax.dynamic_slice_in_dim(inverse_two, first, mine, 0)
    new_basis = combine(rows_mine.T, fresh_all)
    return (new_basis, rayleigh)


def solution(mesh):
    in_specs = (P("space", None, None), P("vec", "space", None, None))
    out_specs = (P("vec", "space", None, None), P())
    return jax.shard_map(local, mesh=mesh, in_specs=in_specs, out_specs=out_specs, check_vma=False)
```

profile of v0, /device:TPU:0, one launch (start us, length us, event | category | flops | bytes accessed | tf_op | source)
XLA Modules:
  0.0 1709.0 jit_solution(7013803013438455873)
XLA Ops:
  7.2 2.6 copy.4
  9.9 38.5 %all-gather.3.cloned.1.call-done = f32[16,1,128,256]{2,0,3,1:T(8,128)} async-done(((f32[8,1,128,256]{2,0,3,1:T(8,128)}), f32[16,1,128,256]{2,0,3,1:T(8,128)}) %all-gather.3.cloned.1.call-update) | async-done | bytes 2097168 | tf_op jit(solution)/shard_map/all_gather | solution.py:53
  48.4 5.2 fusion.26
  53.6 171.0 %psum.70 = f32[16,16]{0,1:T(8,128)S(1)} all-reduce(f32[16,16]{0,1:T(8,128)S(1)} %fusion.26), channel_id=1, replica_groups=mesh['space'=64,'vec'=2] {'space'}, use_global_device_ids=true, to_apply=%region_0.0 | all-reduce | flops 256 | bytes 2048 | tf_op jit(solution)/shard_map/psum | solution.py:54
  224.7 1.5 cholesky.44
  226.2 0.6 compare_reduce_fusion.1
  226.8 0.6 fusion.68
  227.5 1.2 custom-call.6
  228.9 2.1 copy.7
  231.0 3.4 fusion.107
  234.5 2.6 fusion.36
  237.1 162.5 %psum.72 = f32[16,8]{0,1:T(8,128)S(1)} all-reduce(f32[16,8]{0,1:T(8,128)S(1)} %fusion.36), channel_id=1, replica_groups=mesh['space'=64,'vec'=2] {'space'}, use_global_device_ids=true, to_apply=%region_4.7 | all-reduce | flops 128 | bytes 1024 | tf_op jit(solution)/shard_map/psum | solution.py:66
  399.6 1.1 convolution_subtract_fusion
  401.1 0.5 collective-permute-start.3
  402.1 7.1 collective-permute-start
  409.2 0.4 collective-permute-start.1
  409.6 0.3 fusion.99
  410.4 3.1 collective-permute-done.2
  413.4 7.7 collective-permute-done.3
  421.1 0.8 fusion.46
  421.9 2.7 fusion.35
  424.7 7.7 collective-permute-done.1
  432.4 0.8 fusion.41
  433.2 2.6 fusion.37
  435.8 164.5 %all-reduce = (f32[16,8]{0,1:T(8,128)S(1)}, f32[16,8]{0,1:T(8,128)S(1)}) all-reduce(f32[16,8]{0,1:T(8,128)S(1)} %fusion.37, f32[16,8]{0,1:T(8,128)S(1)} %fusion.35), channel_id=1, replica_groups=mesh['space'=64,'vec'=2] {'space'}, use_global_device_ids=true, to_apply=%region_3.6 | all-reduce | flops 256 | bytes 2048 | tf_op jit(solution)/shard_map/psum | solution.py:60
  600.3 4.4 all_gather.10
  604.7 1.2 fusion.17
  605.9 1.3 fusion.18
  607.3 2.6 fusion.34
  609.9 162.5 %psum.74 = f32[16,8]{0,1:T(8,128)S(1)} all-reduce(f32[16,8]{0,1:T(8,128)S(1)} %fusion.34), channel_id=1, replica_groups=mesh['space'=64,'vec'=2] {'space'}, use_global_device_ids=true, to_apply=%region_6.9 | all-reduce | flops 128 | bytes 1024 | tf_op jit(solution)/shard_map/psum | solution.py:66
  772.4 1.1 fusion.13
  773.6 0.6 collective-permute-start.5
  775.0 11.0 collective-permute-done.4
  785.9 7.9 collective-permute-done.5
  793.8 0.8 fusion.51
  794.6 1.0 copy-done.5
  795.6 2.7 fusion.33
  798.3 162.5 %psum.75 = f32[16,8]{0,1:T(8,128)S(1)} all-reduce(f32[16,8]{0,1:T(8,128)S(1)} %fusion.33), channel_id=1, replica_groups=mesh['space'=64,'vec'=2] {'space'}, use_global_device_ids=true, to_apply=%region_7.10 | all-reduce | flops 128 | bytes 1024 | tf_op jit(solution)/shard_map/psum | solution.py:70
  960.8 3.1 fusion.20
  963.9 2.6 fusion.32
  966.5 162.5 %psum.76 = f32[16,8]{0,1:T(8,128)S(1)} all-reduce(f32[16,8]{0,1:T(8,128)S(1)} %fusion.32), channel_id=1, replica_groups=mesh['space'=64,'vec'=2] {'space'}, use_global_device_ids=true, to_apply=%region_8.11 | all-reduce | flops 128 | bytes 1024 | tf_op jit(solution)/shard_map/psum | solution.py:66
  1129.0 1.1 fusion.10
  1130.2 0.5 collective-permute-start.7
  1131.4 11.1 collective-permute-done.6
  1142.5 7.7 collective-permute-done.7
  1150.3 0.8 fusion.56
  1151.0 1.0 copy-done.4
  1152.0 2.7 fusion.31
  1154.7 162.7 %psum.77 = f32[16,8]{0,1:T(8,128)S(1)} all-reduce(f32[16,8]{0,1:T(8,128)S(1)} %fusion.31), channel_id=1, replica_groups=mesh['space'=64,'vec'=2] {'space'}, use_global_device_ids=true, to_apply=%region_9.12 | all-reduce | flops 128 | bytes 1024 | tf_op jit(solution)/shard_map/psum | solution.py:70
  1317.4 2.9 fusion.22
  1320.3 1.0 copy-done.6
  1321.2 2.7 fusion.30
  1323.9 162.5 %psum.78 = f32[16,8]{0,1:T(8,128)S(1)} all-reduce(f32[16,8]{0,1:T(8,128)S(1)} %fusion.30), channel_id=1, replica_groups=mesh['space'=64,'vec'=2] {'space'}, use_global_device_ids=true, to_apply=%region_10.13 | all-reduce | flops 128 | bytes 1024 | tf_op jit(solution)/shard_map/psum | solution.py:73
  1486.4 3.3 fusion.7
  1489.7 0.7 copy.15
  1490.4 28.6 %all-gather.5.cloned.1.call-done = f32[16,1,128,256]{3,0,2,1:T(8,128)} async-done(((f32[8,1,128,256]{3,0,2,1:T(8,128)}), f32[16,1,128,256]{3,0,2,1:T(8,128)}) %all-gather.5.cloned.1.call-update) | async-done | bytes 2097168 | tf_op jit(solution)/shard_map/all_gather | solution.py:75
  1518.9 5.2 fusion.27
  1524.2 171.0 %psum.79 = f32[16,16]{0,1:T(8,128)S(1)} all-reduce(f32[16,16]{0,1:T(8,128)S(1)} %fusion.27), channel_id=1, replica_groups=mesh['space'=64,'vec'=2] {'space'}, use_global_device_ids=true, to_apply=%region_11.14 | all-reduce | flops 256 | bytes 2048 | tf_op jit(solution)/shard_map/psum | solution.py:76
  1695.2 1.5 cholesky.55
  1696.7 0.6 compare_reduce_fusion
  1697.4 0.6 fusion.69
  1698.0 1.2 custom-call.7
  1699.5 1.1 fusion.4
  1700.6 1.3 copy.14
  (50 shorter events, 3.7 us)
Async XLA Ops:
  7.2 2.7 copy-start.9
  7.2 41.2 %all-gather.3.cloned.1.call-start = ((), (), s32[]{:S(2)}) async-start(), calls=%async_computation | async-start | bytes 3145728 | tf_op jit(solution)/shard_map/all_gather | solution.py:53
  9.8 1509.1 %all-gather.5.cloned.1.call-start = ((), (), s32[]{:S(2)}) async-start(), calls=%async_computation.1 | async-start | bytes 3145728 | tf_op jit(solution)/shard_map/all_gather | solution.py:75
  48.4 180.5 %copy-start.7 = (f32[16,1,128,256]{2,0,3,1:T(8,128)S(1)}, f32[16,1,128,256]{2,0,3,1:T(8,128)}, u32[]{:S(2)}) copy-start(f32[16,1,128,256]{2,0,3,1:T(8,128)} %all-gather.3.cloned.1.call-done) | copy-start | bytes 6291460
  401.0 12.4 collective-permute-start.2
  401.1 20.0 %collective-permute-start.3 = (f32[8,1,128,256]{3,0,2,1:T(8,128)S(1)}, f32[8,1,128,256]{3,0,2,1:T(8,128)S(1)}, u32[]{:S(2)}, u32[]{:S(2)}) collective-permute-start(f32[8,1,128,256]{3,0,2,1:T(8,128)S(1)} %bitcast.203), channel_id=1, source_target_pairs={{0,2},{2,4},{4,6},{6,8},{8,10},{10,12},{12,14},{14,16},{16,18},{18... | collective-permute-start | bytes 3145736 | tf_op jit(solution)/shard_map/ppermute | solution.py:18
  402.1 22.6 %collective-permute-start = (f32[8,1,128,256]{3,0,2,1:T(8,128)S(1)}, f32[8,1,128,256]{3,0,2,1:T(8,128)S(1)}, u32[]{:S(2)}, u32[]{:S(2)}) collective-permute-start(f32[8,1,128,256]{3,0,2,1:T(8,128)S(1)} %dynamic-slice_bitcast_fusion), channel_id=1, source_target_pairs={{2,0},{4,2},{6,4},{8,6},{10,8},{12,10},{14,12},{16,14},{18,16},{20... | collective-permute-start | bytes 3145736 | tf_op jit(solution)/shard_map/ppermute | solution.py:19
  409.2 23.2 %collective-permute-start.1 = (f32[8,1,128,256]{3,0,2,1:T(8,128)S(1)}, f32[8,1,128,256]{3,0,2,1:T(8,128)S(1)}, u32[]{:S(2)}, u32[]{:S(2)}) collective-permute-start(f32[8,1,128,256]{3,0,2,1:T(8,128)S(1)} %dynamic-slice_bitcast_fusion), channel_id=1, source_target_pairs={{0,2},{2,4},{4,6},{6,8},{8,10},{10,12},{12,14},{14,16},{16,18},{18... | collective-permute-start | bytes 3145736 | tf_op jit(solution)/shard_map/ppermute | solution.py:18
  421.9 11.3 copy-start.2
  604.7 1.2 copy-start.3
  605.9 1.4 copy-start.1
  607.2 166.3 %copy-start = (f32[8,1,128,256]{3,0,2,1:T(8,128)}, f32[8,1,128,256]{3,0,2,1:T(8,128)S(1)}, u32[]{:S(2)}) copy-start(f32[8,1,128,256]{3,0,2,1:T(8,128)S(1)} %fusion.18) | copy-start | bytes 3145732
  773.5 12.4 collective-permute-start.4
  773.6 20.2 %collective-permute-start.5 = (f32[8,1,128,256]{3,0,2,1:T(8,128)S(1)}, f32[8,1,128,256]{3,0,2,1:T(8,128)S(1)}, u32[]{:S(2)}, u32[]{:S(2)}) collective-permute-start(f32[8,1,128,256]{3,0,2,1:T(8,128)S(1)} %fusion.13), channel_id=1, source_target_pairs={{0,2},{2,4},{4,6},{6,8},{8,10},{10,12},{12,14},{14,16},{16,18},{18... | collective-permute-start | bytes 3145736 | tf_op jit(solution)/shard_map/ppermute | solution.py:18
  794.6 1.0 copy-start.5
  1130.2 12.4 collective-permute-start.6
  1130.2 20.0 %collective-permute-start.7 = (f32[8,1,128,256]{3,0,2,1:T(8,128)S(1)}, f32[8,1,128,256]{3,0,2,1:T(8,128)S(1)}, u32[]{:S(2)}, u32[]{:S(2)}) collective-permute-start(f32[8,1,128,256]{3,0,2,1:T(8,128)S(1)} %fusion.10), channel_id=1, source_target_pairs={{0,2},{2,4},{4,6},{6,8},{8,10},{10,12},{12,14},{14,16},{16,18},{18... | collective-permute-start | bytes 3145736 | tf_op jit(solution)/shard_map/ppermute | solution.py:18
  1151.0 1.0 copy-start.4
  1320.2 1.0 copy-start.6
  1518.9 180.5 %copy-start.8 = (f32[16,1,128,256]{3,0,2,1:T(8,128)S(1)}, f32[16,1,128,256]{3,0,2,1:T(8,128)}, u32[]{:S(2)}) copy-start(f32[16,1,128,256]{3,0,2,1:T(8,128)} %all-gather.5.cloned.1.call-done) | copy-start | bytes 6291460
Sparse Core Ops, SparseCore 0:
  10.2 38.1 all-gather.2
  1489.8 29.0 all-gather.4
where the time goes:
time: 1720 us; the launch traced here: 1710 us
  blocking collectives  1490 us (87%)
  waiting for transfers between devices  123 us (7%)
  matrix products  51.6 us (3%)
    psum x3, blocking collectives, local(): coeff = lax.psum(local_inner(basis_all, correction, scale), 'space')  488 us
    psum x2, blocking collectives, local(): back = lax.psum(local_inner(basis_all, moved, scale), 'space')  325 us
    psum x1, blocking collectives, local(): gram_two = lax.psum(local_inner(fresh_all, fresh_all, scale), 'space')  171 us
    psum x1, blocking collectives, local(): gram = lax.psum(local_inner(whole, whole, scale), 'space')  171 us
    psum x1, blocking collectives, local(): panel = lax.psum(local_inner(basis_all, image, scale), 'space')  165 us
    psum x1, blocking collectives, local(): proj_two = lax.psum(local_inner(basis_all, correction, scale), 'space')  163 us
    all_gather x1, waiting for transfers between devices, local(): whole = lax.all_gather(start_basis, 'vec', axis=0, tiled=True)  38.5 us
  transfers between devices with their start and end apart: 10, of which 10 were waited for; matrix products, arithmetic and copies ran while one was open for 0% of the time, Pallas kernels for 0%

commit v1 on v0

--- a/solution.py
+++ b/solution.py
@@ -70,7 +70,7 @@
         back = lax.psum(local_inner(basis_all, moved, scale), "space")
         update = -resid - (moved - combine(back, basis_all))
         correction = correction + update / shifted
-    proj_two = lax.psum(local_inner(basis_all, correction, scale), "space")
+    proj_two = jnp.sum(lax.all_gather(local_inner(basis_all, correction, scale), "space"), axis=0)
     fresh = correction - combine(proj_two, basis_all)
     fresh_all = lax.all_gather(fresh, "vec", axis=0, tiled=True)
     gram_two = lax.psum(local_inner(fresh_all, fresh_all, scale), "space")

time: 1720 us -> 1650 us (0.959)
  blocking collectives: 1490 us -> 1410 us
    psum x1 -> x0, blocking collectives: 163 us -> none  [local(): proj_two = lax.psum(local_inner(basis_all, correction, scale), 'space')]
    all_gather x0 -> x1, blocking collectives: none -> 88.9 us  [local(): lax.all_gather(local_inner(basis_all, correction, scale), 'space')]
where the time goes in v1:
time: 1650 us; the launch traced here: 1640 us
  blocking collectives  1410 us (85%)
  waiting for transfers between devices  125 us (8%)
  matrix products  51.6 us (3%)
    psum x3, blocking collectives, local(): coeff = lax.psum(local_inner(basis_all, correction, scale), 'space')  488 us
    psum x2, blocking collectives, local(): back = lax.psum(local_inner(basis_all, moved, scale), 'space')  325 us
    psum x1, blocking collectives, local(): gram_two = lax.psum(local_inner(fresh_all, fresh_all, scale), 'space')  171 us
    psum x1, blocking collectives, local(): gram = lax.psum(local_inner(whole, whole, scale), 'space')  171 us
    psum x1, blocking collectives, local(): panel = lax.psum(local_inner(basis_all, image, scale), 'space')  165 us
    all_gather x1, blocking collectives, local(): lax.all_gather(local_inner(basis_all, correction, scale), 'space')  88.9 us
    all_gather x1, waiting for transfers between devices, local(): whole = lax.all_gather(start_basis, 'vec', axis=0, tiled=True)  38.5 us
  transfers between devices with their start and end apart: 10, of which 10 were waited for; matrix products, arithmetic and copies ran while one was open for 0% of the time, Pallas kernels for 0%

profile of v1, /device:TPU:0, one launch (start us, length us, event | category | flops | bytes accessed | tf_op | source)
XLA Modules:
  0.0 1637.2 jit_solution(853357354743582278)
XLA Ops:
  7.2 2.6 copy.18
  9.9 38.5 %all-gather.5.cloned.1.call-done = f32[16,1,128,256]{2,0,3,1:T(8,128)} async-done(((f32[8,1,128,256]{2,0,3,1:T(8,128)}), f32[16,1,128,256]{2,0,3,1:T(8,128)}) %all-gather.5.cloned.1.call-update) | async-done | bytes 2097168 | tf_op jit(solution)/shard_map/all_gather | solution.py:53
  48.4 5.2 fusion.26
  53.6 171.0 %psum.63 = f32[16,16]{0,1:T(8,128)S(1)} all-reduce(f32[16,16]{0,1:T(8,128)S(1)} %fusion.26), channel_id=1, replica_groups=mesh['space'=64,'vec'=2] {'space'}, use_global_device_ids=true, to_apply=%region_0.0 | all-reduce | flops 256 | bytes 2048 | tf_op jit(solution)/shard_map/psum | solution.py:54
  224.7 1.5 cholesky.44
  226.2 0.6 compare_reduce_fusion.1
  226.8 0.6 fusion.69
  227.5 1.2 custom-call.6
  228.9 2.1 copy.21
  231.0 3.4 fusion.108
  234.5 2.6 fusion.37
  237.1 162.5 %psum.65 = f32[16,8]{0,1:T(8,128)S(1)} all-reduce(f32[16,8]{0,1:T(8,128)S(1)} %fusion.37), channel_id=1, replica_groups=mesh['space'=64,'vec'=2] {'space'}, use_global_device_ids=true, to_apply=%region_4.7 | all-reduce | flops 128 | bytes 1024 | tf_op jit(solution)/shard_map/psum | solution.py:66
  399.6 1.1 convolution_subtract_fusion
  401.1 0.5 collective-permute-start.3
  402.1 7.1 collective-permute-start
  409.2 0.4 collective-permute-start.1
  409.6 0.3 fusion.100
  410.4 3.1 collective-permute-done.2
  413.4 7.7 collective-permute-done.3
  421.1 0.8 fusion.47
  421.9 2.7 fusion.36
  424.7 7.7 collective-permute-done.1
  432.4 0.8 fusion.42
  433.2 2.6 fusion.38
  435.8 164.5 %all-reduce = (f32[16,8]{0,1:T(8,128)S(1)}, f32[16,8]{0,1:T(8,128)S(1)}) all-reduce(f32[16,8]{0,1:T(8,128)S(1)} %fusion.38, f32[16,8]{0,1:T(8,128)S(1)} %fusion.36), channel_id=1, replica_groups=mesh['space'=64,'vec'=2] {'space'}, use_global_device_ids=true, to_apply=%region_3.6 | all-reduce | flops 256 | bytes 2048 | tf_op jit(solution)/shard_map/psum | solution.py:60
  600.3 4.4 all_gather.16
  604.7 1.2 fusion.17
  605.9 1.3 fusion.18
  607.3 2.6 fusion.35
  609.9 162.5 %psum.67 = f32[16,8]{0,1:T(8,128)S(1)} all-reduce(f32[16,8]{0,1:T(8,128)S(1)} %fusion.35), channel_id=1, replica_groups=mesh['space'=64,'vec'=2] {'space'}, use_global_device_ids=true, to_apply=%region_6.9 | all-reduce | flops 128 | bytes 1024 | tf_op jit(solution)/shard_map/psum | solution.py:66
  772.4 1.1 fusion.13
  773.6 0.6 collective-permute-start.5
  775.0 11.0 collective-permute-done.4
  785.9 7.9 collective-permute-done.5
  793.8 0.8 fusion.52
  794.6 1.0 copy-done.5
  795.6 2.7 fusion.34
  798.3 162.5 %psum.68 = f32[16,8]{0,1:T(8,128)S(1)} all-reduce(f32[16,8]{0,1:T(8,128)S(1)} %fusion.34), channel_id=1, replica_groups=mesh['space'=64,'vec'=2] {'space'}, use_global_device_ids=true, to_apply=%region_7.10 | all-reduce | flops 128 | bytes 1024 | tf_op jit(solution)/shard_map/psum | solution.py:70
  960.8 3.1 fusion.20
  963.9 2.6 fusion.33
  966.5 162.5 %psum.69 = f32[16,8]{0,1:T(8,128)S(1)} all-reduce(f32[16,8]{0,1:T(8,128)S(1)} %fusion.33), channel_id=1, replica_groups=mesh['space'=64,'vec'=2] {'space'}, use_global_device_ids=true, to_apply=%region_8.11 | all-reduce | flops 128 | bytes 1024 | tf_op jit(solution)/shard_map/psum | solution.py:66
  1129.0 1.1 fusion.10
  1130.2 0.5 collective-permute-start.7
  1131.4 11.1 collective-permute-done.6
  1142.5 7.7 collective-permute-done.7
  1150.3 0.8 fusion.57
  1151.0 1.0 copy-done.4
  1152.0 2.7 fusion.32
  1154.7 162.7 %psum.70 = f32[16,8]{0,1:T(8,128)S(1)} all-reduce(f32[16,8]{0,1:T(8,128)S(1)} %fusion.32), channel_id=1, replica_groups=mesh['space'=64,'vec'=2] {'space'}, use_global_device_ids=true, to_apply=%region_9.12 | all-reduce | flops 128 | bytes 1024 | tf_op jit(solution)/shard_map/psum | solution.py:70
  1317.4 2.9 fusion.22
  1320.3 1.0 copy-done.6
  1321.2 2.7 fusion.31
  1323.9 88.9 %all-gather.1 = f32[64,16,8]{1,2,0:T(8,128)S(1)} all-gather(f32[1,16,8]{1,2,0:T(8,128)S(1)} %fusion.31), channel_id=2, replica_groups=mesh['space'=64,'vec'=2] {'space'}, dimensions={0}, use_global_device_ids=true | all-gather | bytes 33280 | tf_op jit(solution)/shard_map/all_gather | solution.py:73
  1412.8 3.3 fusion.7
  1416.1 0.7 copy.31
  1416.8 30.4 %all-gather.7.cloned.1.call-done = f32[16,1,128,256]{3,0,2,1:T(8,128)} async-done(((f32[8,1,128,256]{3,0,2,1:T(8,128)}), f32[16,1,128,256]{3,0,2,1:T(8,128)}) %all-gather.7.cloned.1.call-update) | async-done | bytes 2097168 | tf_op jit(solution)/shard_map/all_gather | solution.py:75
  1447.2 5.2 fusion.27
  1452.4 171.0 %psum.71 = f32[16,16]{0,1:T(8,128)S(1)} all-reduce(f32[16,16]{0,1:T(8,128)S(1)} %fusion.27), channel_id=1, replica_groups=mesh['space'=64,'vec'=2] {'space'}, use_global_device_ids=true, to_apply=%region_11.14 | all-reduce | flops 256 | bytes 2048 | tf_op jit(solution)/shard_map/psum | solution.py:76
  1623.5 1.5 cholesky.55
  1625.0 0.6 compare_reduce_fusion
  1625.6 0.6 fusion.70
  1626.3 1.2 custom-call.7
  1627.7 1.1 fusion.4
  1628.9 1.3 copy.30
  (51 shorter events, 3.7 us)
Async XLA Ops:
  7.2 2.7 copy-start.9
  7.2 41.2 %all-gather.5.cloned.1.call-start = ((), (), s32[]{:S(2)}) async-start(), calls=%async_computation | async-start | bytes 3145728 | tf_op jit(solution)/shard_map/all_gather | solution.py:53
  9.8 1437.4 %all-gather.7.cloned.1.call-start = ((), (), s32[]{:S(2)}) async-start(), calls=%async_computation.1 | async-start | bytes 3145728 | tf_op jit(solution)/shard_map/all_gather | solution.py:75
  48.4 180.5 %copy-start.7 = (f32[16,1,128,256]{2,0,3,1:T(8,128)S(1)}, f32[16,1,128,256]{2,0,3,1:T(8,128)}, u32[]{:S(2)}) copy-start(f32[16,1,128,256]{2,0,3,1:T(8,128)} %all-gather.5.cloned.1.call-done) | copy-start | bytes 6291460
  401.0 12.4 collective-permute-start.2
  401.1 20.0 %collective-permute-start.3 = (f32[8,1,128,256]{3,0,2,1:T(8,128)S(1)}, f32[8,1,128,256]{3,0,2,1:T(8,128)S(1)}, u32[]{:S(2)}, u32[]{:S(2)}) collective-permute-start(f32[8,1,128,256]{3,0,2,1:T(8,128)S(1)} %bitcast.207), channel_id=1, source_target_pairs={{0,2},{2,4},{4,6},{6,8},{8,10},{10,12},{12,14},{14,16},{16,18},{18... | collective-permute-start | bytes 3145736 | tf_op jit(solution)/shard_map/ppermute | solution.py:18
  402.1 22.6 %collective-permute-start = (f32[8,1,128,256]{3,0,2,1:T(8,128)S(1)}, f32[8,1,128,256]{3,0,2,1:T(8,128)S(1)}, u32[]{:S(2)}, u32[]{:S(2)}) collective-permute-start(f32[8,1,128,256]{3,0,2,1:T(8,128)S(1)} %dynamic-slice_bitcast_fusion), channel_id=1, source_target_pairs={{2,0},{4,2},{6,4},{8,6},{10,8},{12,10},{14,12},{16,14},{18,16},{20... | collective-permute-start | bytes 3145736 | tf_op jit(solution)/shard_map/ppermute | solution.py:19
  409.2 23.2 %collective-permute-start.1 = (f32[8,1,128,256]{3,0,2,1:T(8,128)S(1)}, f32[8,1,128,256]{3,0,2,1:T(8,128)S(1)}, u32[]{:S(2)}, u32[]{:S(2)}) collective-permute-start(f32[8,1,128,256]{3,0,2,1:T(8,128)S(1)} %dynamic-slice_bitcast_fusion), channel_id=1, source_target_pairs={{0,2},{2,4},{4,6},{6,8},{8,10},{10,12},{12,14},{14,16},{16,18},{18... | collective-permute-start | bytes 3145736 | tf_op jit(solution)/shard_map/ppermute | solution.py:18
  421.9 11.3 copy-start.2
  604.7 1.2 copy-start.3
  605.9 1.4 copy-start.1
  607.2 166.3 %copy-start = (f32[8,1,128,256]{3,0,2,1:T(8,128)}, f32[8,1,128,256]{3,0,2,1:T(8,128)S(1)}, u32[]{:S(2)}) copy-start(f32[8,1,128,256]{3,0,2,1:T(8,128)S(1)} %fusion.18) | copy-start | bytes 3145732
  773.5 12.4 collective-permute-start.4
  773.6 20.2 %collective-permute-start.5 = (f32[8,1,128,256]{3,0,2,1:T(8,128)S(1)}, f32[8,1,128,256]{3,0,2,1:T(8,128)S(1)}, u32[]{:S(2)}, u32[]{:S(2)}) collective-permute-start(f32[8,1,128,256]{3,0,2,1:T(8,128)S(1)} %fusion.13), channel_id=1, source_target_pairs={{0,2},{2,4},{4,6},{6,8},{8,10},{10,12},{12,14},{14,16},{16,18},{18... | collective-permute-start | bytes 3145736 | tf_op jit(solution)/shard_map/ppermute | solution.py:18
  794.6 1.0 copy-start.5
  1130.2 12.4 collective-permute-start.6
  1130.2 20.0 %collective-permute-start.7 = (f32[8,1,128,256]{3,0,2,1:T(8,128)S(1)}, f32[8,1,128,256]{3,0,2,1:T(8,128)S(1)}, u32[]{:S(2)}, u32[]{:S(2)}) collective-permute-start(f32[8,1,128,256]{3,0,2,1:T(8,128)S(1)} %fusion.10), channel_id=1, source_target_pairs={{0,2},{2,4},{4,6},{6,8},{8,10},{10,12},{12,14},{14,16},{16,18},{18... | collective-permute-start | bytes 3145736 | tf_op jit(solution)/shard_map/ppermute | solution.py:18
  1151.0 1.0 copy-start.4
  1320.2 1.0 copy-start.6
  1447.2 180.5 %copy-start.8 = (f32[16,1,128,256]{3,0,2,1:T(8,128)S(1)}, f32[16,1,128,256]{3,0,2,1:T(8,128)}, u32[]{:S(2)}) copy-start(f32[16,1,128,256]{3,0,2,1:T(8,128)} %all-gather.7.cloned.1.call-done) | copy-start | bytes 6291460
Sparse Core Ops, SparseCore 0:
  10.2 38.1 all-gather.4
  1416.3 30.9 all-gather.6
